TPU v7x, 512 devices: a whole 4x8x8 slice. The times are simulated.
512 devices in a mesh: segment: 16 (over z, core), mp: 32 (over y, x).
Axes of the slice: x: 4, y: 8, z: 8, core: 2. Of those that a mesh axis runs over, the one named last changes fastest.
Arguments:
- rows: bfloat16 [16, 2, 128, 8192], P('segment', None, None, 'mp'), may hold values from -6 to 6
- carry: bfloat16 [16, 128, 8192], P('segment', None, 'mp'), may hold values from -6 to 6
- weights: bfloat16 [16, 2, 8192, 4096], P('segment', None, None, 'mp'), may hold values from -1.1932427 to 1.1932427
- neighbours: int32 [16, 2, 2, 2], P('segment'), may hold values from 0 to 7, all different within a row
Outputs:
- passed: bfloat16 [16, 128, 8192], P('segment', None, 'mp')
- returned: bfloat16 [16, 128, 8192], P('segment', None, 'mp')
- kv_grad: bfloat16 [1024, 2, 4096], P(None, None, 'mp')
Inputs may be any that keep to these rules, and one draw needn't show every extreme that they name: Each group's 2 neighbours are different pool blocks; pool blocks are numbered by encoder segment in order, then by row.
All inputs are finite; a program needn't handle non-finite values.
Results may differ from a plain program's by a relative error of at most 0.02.
The roundings to bfloat16 on the way count: a program that leaves them out, or rounds other values in their place, can miss the bound.
Values may be sent and summed in bfloat16 or wider, within the bound.
No kernel may reach another device: no remote copies, remote signals or barrier semaphores. Data moves between devices by JAX's collectives and lax.ppermute only.
A program may use at most 64 MiB of HBM per device.

v0:
```python
import math
import jax
import jax.numpy as jnp
from jax import lax
from jax.sharding import PartitionSpec as P

GROUP = 64
NBLEN = 128
NEIGH = 2


def from_behind(x, axis, by):
    devices = lax.axis_size(axis)
    return lax.ppermute(x, axis, [(i, (i + by) % devices) for i in range(devices)])


def attend(queries, key_rows, score_scale):
    scores = (
        jnp.einsum("cqd,ckd->cqk", queries, key_rows, preferred_element_type=jnp.float32)
        * score_scale
    )
    soft = jax.nn.softmax(scores, axis=-1)
    return (soft, soft.astype(jnp.bfloat16))


def attend_back(queries, key_rows, value_rows, soft, rounded, upstream, score_scale):
    d_soft = jnp.einsum("cqd,ckd->cqk", upstream, value_rows, preferred_element_type=jnp.float32)
    grad_values = jnp.einsum("cqk,cqd->ckd", rounded, upstream, preferred_element_type=jnp.float32)
    d_scores = soft * (d_soft - jnp.sum(d_soft * soft, axis=-1, keepdims=True))
    grad_queries = (
        jnp.einsum("cqk,ckd->cqd", d_scores, key_rows.astype(jnp.float32)) * score_scale
    ).astype(jnp.bfloat16)
    grad_keys = jnp.einsum("cqk,cqd->ckd", d_scores, queries.astype(jnp.float32)) * score_scale
    return (grad_queries, grad_keys, grad_values)


def head_sum(term, axis):
    devices = lax.axis_size(axis)
    parts = term.astype(jnp.bfloat16).reshape(devices, term.shape[0] // devices, term.shape[1])
    moved = lax.all_to_all(parts, axis, 0, 0, tiled=True)
    return jnp.sum(moved.astype(jnp.float32), axis=0).T


def segment_sum(contrib, axis):
    devices = lax.axis_size(axis)
    parts = contrib.reshape(devices, contrib.shape[0] // devices, contrib.shape[1])
    moved = lax.all_to_all(parts, axis, 0, 0, tiled=True)
    summed = jnp.sum(moved.astype(jnp.float32), axis=0).astype(jnp.bfloat16)
    spread = jnp.broadcast_to(summed[None], (devices,) + summed.shape)
    return lax.all_to_all(spread, axis, 0, 0, tiled=True).reshape(contrib.shape)


def per_device(rows, carry, weights, neighbours):
    segments = lax.axis_size("segment")
    encoders = segments // 4
    first_encoder = segments - encoders
    is_encoder = lax.axis_index("segment") >= first_encoder
    local_rows = rows[0]
    local_carry = carry[0]
    full_rows, full_carry = (
        lax.all_gather(local_rows, "mp", axis=2, tiled=True),
        lax.all_gather(local_carry, "mp", axis=1, tiled=True),
    )
    tokens = local_rows.shape[1]
    width = full_rows.shape[2]
    head = weights.shape[3]
    w_query = weights[0, 0]
    w_out = weights[0, 1]

    def encode():
        flat = full_rows.reshape(2 * tokens, width)
        keyval = jnp.concatenate(
            [
                jnp.dot(flat, w_query, preferred_element_type=jnp.float32),
                jnp.dot(flat, w_out, preferred_element_type=jnp.float32),
            ],
            axis=-1,
        ).astype(jnp.bfloat16)
        return (keyval, jnp.zeros((2 * tokens, head), jnp.bfloat16))

    def decode():
        queries = jnp.dot(
            full_rows.reshape(2 * tokens, width), w_query, preferred_element_type=jnp.float32
        ).astype(jnp.bfloat16)
        return (jnp.zeros((2 * tokens, 2 * head), jnp.bfloat16), queries)

    encoded, queries = lax.cond(is_encoder, encode, decode)
    per_encoder = 2 * tokens // NBLEN
    pool_blocks = encoders * per_encoder
    collected = lax.all_gather(encoded, "segment", axis=0, tiled=True)
    pool = collected[first_encoder * 2 * tokens :].reshape(pool_blocks, NBLEN, 2 * head)
    groups = tokens // GROUP
    local_nbr = neighbours[0]
    score_scale = 1.0 / math.sqrt(head)
    query_blocks = queries.reshape(2, groups, GROUP, head)

    def fetch(batch):
        picked = pool[local_nbr[batch]].reshape(groups, NEIGH * NBLEN, 2 * head)
        return (picked[..., :head], picked[..., head:])

    keys_fwd, values_fwd = fetch(0)
    soft_fwd, rounded_fwd = attend(query_blocks[0], keys_fwd, score_scale)
    mixed = jnp.einsum(
        "cqk,ckd->cqd", rounded_fwd, values_fwd, preferred_element_type=jnp.float32
    ).astype(jnp.bfloat16)
    mixed_flat = mixed.reshape(tokens, head)
    piece = w_out
    out_sum = head_sum(
        lax.dot_general(
            piece, mixed_flat, (((1,), (1,)), ((), ())), preferred_element_type=jnp.float32
        ),
        "mp",
    )
    forward_rows = (local_rows[0].astype(jnp.float32) + out_sum).astype(jnp.bfloat16)
    forward_rows = jnp.where(is_encoder, local_carry, forward_rows)
    passed = from_behind(forward_rows[None], "segment", 1)
    upstream = (
        jnp.dot(full_carry, w_out, preferred_element_type=jnp.float32)
        .astype(jnp.bfloat16)
        .reshape(groups, GROUP, head)
    )
    keys_back, values_back = fetch(1)
    soft_back, rounded_back = attend(query_blocks[1], keys_back, score_scale)
    grad_queries, grad_keys, grad_values = attend_back(
        query_blocks[1], keys_back, values_back, soft_back, rounded_back, upstream, score_scale
    )
    grad_flat = grad_queries.reshape(tokens, head)
    piece = w_query
    grad_input = head_sum(
        lax.dot_general(
            piece, grad_flat, (((1,), (1,)), ((), ())), preferred_element_type=jnp.float32
        ),
        "mp",
    )
    back = local_carry.astype(jnp.float32) + grad_input
    back_rows = jnp.where(is_encoder, local_carry, back.astype(jnp.bfloat16))
    returned = from_behind(back_rows[None], "segment", -1)
    onehot = (
        local_nbr[1][..., None] == jnp.arange(pool_blocks, dtype=jnp.int32)[None, None, :]
    ).astype(jnp.float32)
    grad_keyval = jnp.concatenate([grad_keys, grad_values], axis=-1).reshape(
        groups, NEIGH, NBLEN, 2 * head
    )
    contrib = jnp.einsum("cbp,cbrf->prf", onehot, grad_keyval)
    contrib = jnp.where(is_encoder, jnp.zeros_like(contrib), contrib)
    pooled = segment_sum(
        contrib.astype(jnp.bfloat16).reshape(pool_blocks * NBLEN, 2 * head), "segment"
    )
    kv_grad = pooled.reshape(pool_blocks * NBLEN, 2, head)
    return (passed, returned, kv_grad)


def solution(mesh):
    placed = (
        P("segment", None, None, "mp"),
        P("segment", None, "mp"),
        P("segment", None, None, "mp"),
        P("segment", None, None, None),
    )
    return jax.shard_map(
        per_device,
        mesh=mesh,
        in_specs=placed,
        out_specs=(P("segment", None, "mp"), P("segment", None, "mp"), P(None, None, "mp")),
        check_vma=False,
    )
```

profile of v0, /device:TPU:1, one launch (start us, length us, event | category | flops | bytes accessed | tf_op | source)
XLA Modules:
  0.0 407.9 jit_solution(1906226420023038693)
XLA Ops:
  8.7 3.8 slice_bitcast_fusion
  12.5 89.2 %all-gather.8.cloned.1.call-done = bf16[1,2,128,8192]{3,2,1,0:T(8,128)(2,1)} async-done(((bf16[1,2,128,256]{3,2,1,0:T(8,128)(2,1)}), bf16[1,2,128,8192]{3,2,1,0:T(8,128)(2,1)}) %all-gather.8.cloned.1.call-update) | async-done | bytes 4194320 | tf_op jit(solution)/shard_map/all_gather | solution.py:61
  101.8 3.5 conditional.1
  101.8 3.4 convolution_convert_fusion
  106.2 79.5 %all-gather.10.cloned.1.call-done = bf16[1,128,8192]{2,1,0:T(8,128)(2,1)} async-done(((bf16[1,128,256]{2,1,0:T(8,128)(2,1)}), bf16[1,128,8192]{2,1,0:T(8,128)(2,1)}) %all-gather.10.cloned.1.call-update) | async-done | bytes 2097168 | tf_op jit(solution)/shard_map/all_gather | solution.py:62
  185.7 2.9 fusion.11
  188.6 45.9 %all-gather.6.cloned.1.call-done = bf16[4096,256]{1,0:T(8,128)(2,1)} async-done(((bf16[256,256]{1,0:T(8,128)(2,1)}), bf16[4096,256]{1,0:T(8,128)(2,1)}) %all-gather.6.cloned.1.call-update) | async-done | bytes 2097168 | tf_op jit(solution)/shard_map/all_gather | solution.py:90
  234.5 1.1 slice.67
  238.8 0.9 copy.19
  239.7 4.4 %all-to-all-start.2 = ((bf16[16,64,256]{2,1,0:T(8,128)(2,1)}), bf16[16,64,256]{2,1,0:T(8,128)(2,1)S(1)}, u32[]{:S(2)}, u32[]{:S(2)}) async-start(bf16[16,64,256]{2,1,0:T(8,128)(2,1)} %bitcast.28), calls=%async_computation.2 | async-start | bytes 1048576 | tf_op jit(solution)/shard_map/all_to_all | solution.py:47
  244.5 2.3 convolution_convert_fusion.3
  246.8 1.6 copy.25
  248.4 13.1 %all-to-all-done.2 = bf16[16,64,256]{2,1,0:T(8,128)(2,1)S(1)} async-done(((bf16[16,64,256]{2,1,0:T(8,128)(2,1)}), bf16[16,64,256]{2,1,0:T(8,128)(2,1)S(1)}, u32[]{:S(2)}, u32[]{:S(2)}) %all-to-all-start.2) | async-done | bytes 524320 | tf_op jit(solution)/shard_map/all_to_all | solution.py:47
  261.5 9.3 %all-to-all-start.1 = ((bf16[32,256,128]{1,2,0:T(8,128)(2,1)}), bf16[32,256,128]{1,2,0:T(8,128)(2,1)S(1)}, u32[]{:S(2)}, u32[]{:S(2)}) async-start(bf16[32,256,128]{1,2,0:T(8,128)(2,1)} %bitcast.105), calls=%async_computation.1 | async-start | bytes 4194304 | tf_op jit(solution)/shard_map/all_to_all | solution.py:40
  272.1 2.3 convolution_convert_fusion.4
  274.4 1.6 copy.26
  276.0 45.4 %all-to-all-done.1 = bf16[32,256,128]{1,2,0:T(8,128)(2,1)S(1)} async-done(((bf16[32,256,128]{1,2,0:T(8,128)(2,1)}), bf16[32,256,128]{1,2,0:T(8,128)(2,1)S(1)}, u32[]{:S(2)}, u32[]{:S(2)}) %all-to-all-start.1) | async-done | bytes 2097184 | tf_op jit(solution)/shard_map/all_to_all | solution.py:40
  321.4 5.1 %all-to-all-start = ((bf16[32,256,128]{1,2,0:T(8,128)(2,1)}), bf16[32,256,128]{1,2,0:T(8,128)(2,1)}, u32[]{:S(2)}, u32[]{:S(2)}) async-start(bf16[32,256,128]{1,2,0:T(8,128)(2,1)} %bitcast.106), calls=%async_computation | async-start | bytes 4194304 | tf_op jit(solution)/shard_map/all_to_all | solution.py:40
  326.7 48.3 %all-to-all-done = bf16[32,256,128]{1,2,0:T(8,128)(2,1)} async-done(((bf16[32,256,128]{1,2,0:T(8,128)(2,1)}), bf16[32,256,128]{1,2,0:T(8,128)(2,1)}, u32[]{:S(2)}, u32[]{:S(2)}) %all-to-all-start) | async-done | bytes 2097184 | tf_op jit(solution)/shard_map/all_to_all | solution.py:40
  375.9 6.0 %all-to-all-start.3 = ((bf16[16,64,256]{2,1,0:T(8,128)(2,1)}), bf16[16,64,256]{2,1,0:T(8,128)(2,1)S(1)}, u32[]{:S(2)}, u32[]{:S(2)}) async-start(bf16[16,64,256]{2,1,0:T(8,128)(2,1)} %broadcast_in_dim.11), calls=%async_computation.3 | async-start | bytes 1048576 | tf_op jit(solution)/shard_map/all_to_all | solution.py:50
  382.2 1.9 convert_reduce_fusion.1
  384.1 1.7 collective-permute-start
  385.8 13.4 %all-to-all-done.3 = bf16[16,64,256]{2,1,0:T(8,128)(2,1)S(1)} async-done(((bf16[16,64,256]{2,1,0:T(8,128)(2,1)}), bf16[16,64,256]{2,1,0:T(8,128)(2,1)S(1)}, u32[]{:S(2)}, u32[]{:S(2)}) %all-to-all-start.3) | async-done | bytes 524320 | tf_op jit(solution)/shard_map/all_to_all | solution.py:50
  399.2 0.9 reshape_reshape.7
  (47 shorter events, 9.7 us)
Async XLA Ops:
  7.2 94.6 %all-gather.8.cloned.1.call-start = ((), (), s32[]{:S(2)}) async-start(), calls=%async_computation.5 | async-start | bytes 4325376 | tf_op jit(solution)/shard_map/all_gather | solution.py:61
  7.9 177.8 %all-gather.10.cloned.1.call-start = ((), (), s32[]{:S(2)}) async-start(), calls=%async_computation.6 | async-start | bytes 2162688 | tf_op jit(solution)/shard_map/all_gather | solution.py:62
  8.6 225.9 %all-gather.6.cloned.1.call-start = ((), (), s32[]{:S(2)}) async-start(), calls=%async_computation.4 | async-start | bytes 2228224 | tf_op jit(solution)/shard_map/all_gather | solution.py:90
  101.8 4.2 %copy-start.4 = (s32[1,2,2,2]{3,2,1,0:T(2,128)S(1)}, s32[1,2,2,2]{3,2,1,0:T(2,128)}, u32[]{:S(2)}) copy-start(s32[1,2,2,2]{3,2,1,0:T(2,128)} %param.9) | copy-start | bytes 100
  105.3 0.7 copy-start.1
  239.7 21.7 %all-to-all-start.2 = ((bf16[16,64,256]{2,1,0:T(8,128)(2,1)}), bf16[16,64,256]{2,1,0:T(8,128)(2,1)S(1)}, u32[]{:S(2)}, u32[]{:S(2)}) async-start(bf16[16,64,256]{2,1,0:T(8,128)(2,1)} %bitcast.28), calls=%async_computation.2 | async-start | bytes 1048576 | tf_op jit(solution)/shard_map/all_to_all | solution.py:47
  261.5 60.0 %all-to-all-start.1 = ((bf16[32,256,128]{1,2,0:T(8,128)(2,1)}), bf16[32,256,128]{1,2,0:T(8,128)(2,1)S(1)}, u32[]{:S(2)}, u32[]{:S(2)}) async-start(bf16[32,256,128]{1,2,0:T(8,128)(2,1)} %bitcast.105), calls=%async_computation.1 | async-start | bytes 4194304 | tf_op jit(solution)/shard_map/all_to_all | solution.py:40
  321.4 53.6 %all-to-all-start = ((bf16[32,256,128]{1,2,0:T(8,128)(2,1)}), bf16[32,256,128]{1,2,0:T(8,128)(2,1)}, u32[]{:S(2)}, u32[]{:S(2)}) async-start(bf16[32,256,128]{1,2,0:T(8,128)(2,1)} %bitcast.106), calls=%async_computation | async-start | bytes 4194304 | tf_op jit(solution)/shard_map/all_to_all | solution.py:40
  375.9 23.4 %all-to-all-start.3 = ((bf16[16,64,256]{2,1,0:T(8,128)(2,1)}), bf16[16,64,256]{2,1,0:T(8,128)(2,1)S(1)}, u32[]{:S(2)}, u32[]{:S(2)}) async-start(bf16[16,64,256]{2,1,0:T(8,128)(2,1)} %broadcast_in_dim.11), calls=%async_computation.3 | async-start | bytes 1048576 | tf_op jit(solution)/shard_map/all_to_all | solution.py:50
  381.9 2.2 copy-start.2
  381.9 2.2 copy-start.3
  384.1 16.0 %collective-permute-start = (bf16[1,128,256]{2,1,0:T(8,128)(2,1)S(1)}, bf16[1,128,256]{2,1,0:T(8,128)(2,1)S(1)}, u32[]{:S(2)}, u32[]{:S(2)}) collective-permute-start(bf16[1,128,256]{2,1,0:T(8,128)(2,1)S(1)} %get-tuple-element.53), channel_id=1, source_target_pairs={{0,32},{32,64},{64,96},{96,128},{128,160},{160,192},{192,224},{224... | collective-permute-start | bytes 196616 | tf_op jit(solution)/shard_map/ppermute | solution.py:14
  385.8 14.4 %collective-permute-start.1 = (bf16[1,128,256]{2,1,0:T(8,128)(2,1)S(1)}, bf16[1,128,256]{2,1,0:T(8,128)(2,1)S(1)}, u32[]{:S(2)}, u32[]{:S(2)}) collective-permute-start(bf16[1,128,256]{2,1,0:T(8,128)(2,1)S(1)} %get-tuple-element.52), channel_id=1, source_target_pairs={{0,480},{32,0},{64,32},{96,64},{128,96},{160,128},{192,160},{224,1... | collective-permute-start | bytes 196616 | tf_op jit(solution)/shard_map/ppermute | solution.py:14
Sparse Core Ops, SparseCore 0:
  11.0 90.6 all-gather.7
  104.8 80.8 all-gather.9
  188.4 46.0 all-gather.5
where the time goes:
time: 409 us; the launch traced here: 408 us
  waiting for transfers between devices  336 us (82%)
  starting transfers between devices  26.6 us (7%)
  local copies, waits for them, and re-layouts  14.6 us (4%)
  between operations  14 us (3%)
  matrix products  13.5 us (3%)
    all_to_all x2, waiting for transfers between devices, head_sum(): moved = lax.all_to_all(parts, axis, 0, 0, tiled=True)  93.8 us
    all_gather x1, waiting for transfers between devices, per_device(): lax.all_gather(local_rows, 'mp', axis=2, tiled=True)  89.2 us
    all_gather x1, waiting for transfers between devices, per_device(): lax.all_gather(local_carry, 'mp', axis=1, tiled=True)  79.5 us
    all_gather x1, waiting for transfers between devices, per_device(): collected = lax.all_gather(encoded, 'segment', axis=0, tiled=True)  45.9 us
    all_to_all x2, starting transfers between devices, head_sum(): moved = lax.all_to_all(parts, axis, 0, 0, tiled=True)  14.4 us
    all_to_all x1, waiting for transfers between devices, segment_sum(): return lax.all_to_all(spread, axis, 0, 0, tiled=True).reshape(contrib.shape)  13.4 us
    all_to_all x1, waiting for transfers between devices, segment_sum(): moved = lax.all_to_all(parts, axis, 0, 0, tiled=True)  13.1 us
  transfers between devices with their start and end apart: 9, of which 7 were waited for; matrix products, arithmetic and copies ran while one was open for 6% of the time, Pallas kernels for 0%

commit v1 on v0

--- a/solution.py
+++ b/solution.py
@@ -7,6 +7,12 @@
 GROUP = 64
 NBLEN = 128
 NEIGH = 2
+
+
+def tiled_gather(x, axis, dim):
+    length = lax.axis_size(axis)
+    repeats = [length if d == dim else 1 for d in range(x.ndim)]
+    return lax.all_to_all(jnp.tile(x, repeats), axis, split_axis=dim, concat_axis=dim, tiled=True)
 
 
 def from_behind(x, axis, by):
@@ -87,7 +93,7 @@
     encoded, queries = lax.cond(is_encoder, encode, decode)
     per_encoder = 2 * tokens // NBLEN
     pool_blocks = encoders * per_encoder
-    collected = lax.all_gather(encoded, "segment", axis=0, tiled=True)
+    collected = tiled_gather(encoded, "segment", 0)
     pool = collected[first_encoder * 2 * tokens :].reshape(pool_blocks, NBLEN, 2 * head)
     groups = tokens // GROUP
     local_nbr = neighbours[0]

time: 409 us -> 367 us (0.90)
  waiting for transfers between devices: 336 us -> 277 us
  starting transfers between devices: 26.6 us -> 44.1 us
    all_gather x1 -> x0, waiting for transfers between devices: 45.9 us -> none  [per_device(): collected = lax.all_gather(encoded, 'segment', axis=0, tiled=True)]
    all_gather x1, waiting for transfers between devices: 79.5 us -> 66 us  [per_device(): lax.all_gather(local_carry, 'mp', axis=1, tiled=True)]
    all_to_all x0 -> x1, starting transfers between devices: none -> 12.7 us  [tiled_gather(): lax.all_to_all(jnp.tile(x, repeats), axis, split_axis=dim, concat_axis=di...]
    all_to_all x1, starting transfers between devices: 4.42 us -> 10.9 us  [segment_sum(): moved = lax.all_to_all(parts, axis, 0, 0, tiled=True)]
  transfers between devices with their start and end apart: 9 -> 9, of which waited for: 7 -> 6; matrix products, arithmetic and copies ran while one was open for 6% -> 7% of each run, Pallas kernels for 0% -> 0%
where the time goes in v1:
time: 367 us; the launch traced here: 366 us
  waiting for transfers between devices  277 us (75%)
  starting transfers between devices  44.1 us (12%)
  local copies, waits for them, and re-layouts  14.5 us (4%)
  between operations  14.2 us (4%)
  matrix products  13.4 us (4%)
    all_to_all x2, waiting for transfers between devices, head_sum(): moved = lax.all_to_all(parts, axis, 0, 0, tiled=True)  93.8 us
    all_gather x1, waiting for transfers between devices, per_device(): lax.all_gather(local_rows, 'mp', axis=2, tiled=True)  89.3 us
    all_gather x1, waiting for transfers between devices, per_device(): lax.all_gather(local_carry, 'mp', axis=1, tiled=True)  66 us
    all_to_all x1, waiting for transfers between devices, segment_sum(): return lax.all_to_all(spread, axis, 0, 0, tiled=True).reshape(contrib.shape)  13.4 us
    all_to_all x1, waiting for transfers between devices, segment_sum(): moved = lax.all_to_all(parts, axis, 0, 0, tiled=True)  13.1 us
    all_to_all x2, starting transfers between devices, head_sum(): moved = lax.all_to_all(parts, axis, 0, 0, tiled=True)  12.7 us
    all_to_all x1, starting transfers between devices, tiled_gather(): lax.all_to_all(jnp.tile(x, repeats), axis, split_axis=dim, concat_axis=di...  12.7 us
    all_to_all x1, starting transfers between devices, segment_sum(): moved = lax.all_to_all(parts, axis, 0, 0, tiled=True)  10.9 us
  transfers between devices with their start and end apart: 9, of which 6 were waited for; matrix products, arithmetic and copies ran while one was open for 7% of the time, Pallas kernels for 0%

profile of v1, /device:TPU:1, one launch (start us, length us, event | category | flops | bytes accessed | tf_op | source)
XLA Modules:
  0.0 366.2 jit_solution(6764382085983045670)
XLA Ops:
  8.6 3.8 %slice_bitcast_fusion = (bf16[8192,128]{1,0:T(8,128)(2,1)}, bf16[8192,128]{1,0:T(8,128)(2,1)S(1)}) fusion(bf16[1,2,8192,128]{3,2,1,0:T(8,128)(2,1)} %param.8), kind=kLoop, calls=%fused_computation.16 | loop fusion | bytes 8388608 | tf_op jit(solution)/shard_map/squeeze | solution.py:74
  12.5 89.3 %all-gather.5.cloned.1.call-done = bf16[1,2,128,8192]{3,2,1,0:T(8,128)(2,1)} async-done(((bf16[1,2,128,256]{3,2,1,0:T(8,128)(2,1)}), bf16[1,2,128,8192]{3,2,1,0:T(8,128)(2,1)}) %all-gather.5.cloned.1.call-update) | async-done | bytes 4194320 | tf_op jit(solution)/shard_map/all_gather | solution.py:67
  101.8 3.5 conditional.1
  101.8 3.4 convolution_convert_fusion
  105.3 1.6 tile.2
  106.8 12.7 %all-to-all-start = ((bf16[16,256,256]{2,1,0:T(8,128)(2,1)}), bf16[16,256,256]{2,1,0:T(8,128)(2,1)S(1)}, u32[]{:S(2)}, u32[]{:S(2)}) async-start(bf16[16,256,256]{2,1,0:T(8,128)(2,1)} %tile.2), calls=%async_computation | async-start | bytes 4194304 | tf_op jit(solution)/shard_map/all_to_all | solution.py:15
  119.8 66.0 %all-gather.7.cloned.1.call-done = bf16[1,128,8192]{2,1,0:T(8,128)(2,1)} async-done(((bf16[1,128,256]{2,1,0:T(8,128)(2,1)}), bf16[1,128,8192]{2,1,0:T(8,128)(2,1)}) %all-gather.7.cloned.1.call-update) | async-done | bytes 2097168 | tf_op jit(solution)/shard_map/all_gather | solution.py:68
  185.8 2.9 fusion.11
  192.0 0.9 copy.19
  192.9 10.9 %all-to-all-start.3 = ((bf16[16,64,256]{2,1,0:T(8,128)(2,1)}), bf16[16,64,256]{2,1,0:T(8,128)(2,1)S(1)}, u32[]{:S(2)}, u32[]{:S(2)}) async-start(bf16[16,64,256]{2,1,0:T(8,128)(2,1)} %bitcast.28), calls=%async_computation.3 | async-start | bytes 1048576 | tf_op jit(solution)/shard_map/all_to_all | solution.py:53
  204.1 2.3 convolution_convert_fusion.3
  206.4 1.6 copy.25
  208.0 13.1 %all-to-all-done.3 = bf16[16,64,256]{2,1,0:T(8,128)(2,1)S(1)} async-done(((bf16[16,64,256]{2,1,0:T(8,128)(2,1)}), bf16[16,64,256]{2,1,0:T(8,128)(2,1)S(1)}, u32[]{:S(2)}, u32[]{:S(2)}) %all-to-all-start.3) | async-done | bytes 524320 | tf_op jit(solution)/shard_map/all_to_all | solution.py:53
  221.1 7.6 %all-to-all-start.2 = ((bf16[32,256,128]{1,2,0:T(8,128)(2,1)}), bf16[32,256,128]{1,2,0:T(8,128)(2,1)S(1)}, u32[]{:S(2)}, u32[]{:S(2)}) async-start(bf16[32,256,128]{1,2,0:T(8,128)(2,1)} %bitcast.105), calls=%async_computation.2 | async-start | bytes 4194304 | tf_op jit(solution)/shard_map/all_to_all | solution.py:46
  230.0 2.3 convolution_convert_fusion.4
  232.3 1.6 copy.26
  234.0 45.4 %all-to-all-done.2 = bf16[32,256,128]{1,2,0:T(8,128)(2,1)S(1)} async-done(((bf16[32,256,128]{1,2,0:T(8,128)(2,1)}), bf16[32,256,128]{1,2,0:T(8,128)(2,1)S(1)}, u32[]{:S(2)}, u32[]{:S(2)}) %all-to-all-start.2) | async-done | bytes 2097184 | tf_op jit(solution)/shard_map/all_to_all | solution.py:46
  279.4 5.1 %all-to-all-start.1 = ((bf16[32,256,128]{1,2,0:T(8,128)(2,1)}), bf16[32,256,128]{1,2,0:T(8,128)(2,1)}, u32[]{:S(2)}, u32[]{:S(2)}) async-start(bf16[32,256,128]{1,2,0:T(8,128)(2,1)} %bitcast.106), calls=%async_computation.1 | async-start | bytes 4194304 | tf_op jit(solution)/shard_map/all_to_all | solution.py:46
  284.6 48.3 %all-to-all-done.1 = bf16[32,256,128]{1,2,0:T(8,128)(2,1)} async-done(((bf16[32,256,128]{1,2,0:T(8,128)(2,1)}), bf16[32,256,128]{1,2,0:T(8,128)(2,1)}, u32[]{:S(2)}, u32[]{:S(2)}) %all-to-all-start.1) | async-done | bytes 2097184 | tf_op jit(solution)/shard_map/all_to_all | solution.py:46
  333.8 6.0 %all-to-all-start.4 = ((bf16[16,64,256]{2,1,0:T(8,128)(2,1)}), bf16[16,64,256]{2,1,0:T(8,128)(2,1)S(1)}, u32[]{:S(2)}, u32[]{:S(2)}) async-start(bf16[16,64,256]{2,1,0:T(8,128)(2,1)} %broadcast_in_dim.11), calls=%async_computation.4 | async-start | bytes 1048576 | tf_op jit(solution)/shard_map/all_to_all | solution.py:56
  340.2 1.9 convert_reduce_fusion.1
  342.1 1.7 collective-permute-start
  343.8 13.4 %all-to-all-done.4 = bf16[16,64,256]{2,1,0:T(8,128)(2,1)S(1)} async-done(((bf16[16,64,256]{2,1,0:T(8,128)(2,1)}), bf16[16,64,256]{2,1,0:T(8,128)(2,1)S(1)}, u32[]{:S(2)}, u32[]{:S(2)}) %all-to-all-start.4) | async-done | bytes 524320 | tf_op jit(solution)/shard_map/all_to_all | solution.py:56
  357.2 0.9 reshape_reshape.7
  (45 shorter events, 9.0 us)
Async XLA Ops:
  7.2 94.6 %all-gather.5.cloned.1.call-start = ((), (), s32[]{:S(2)}) async-start(), calls=%async_computation.5 | async-start | bytes 4325376 | tf_op jit(solution)/shard_map/all_gather | solution.py:67
  7.9 177.9 %all-gather.7.cloned.1.call-start = ((), (), s32[]{:S(2)}) async-start(), calls=%async_computation.6 | async-start | bytes 2162688 | tf_op jit(solution)/shard_map/all_gather | solution.py:68
  106.8 12.7 %copy-start.3 = (s32[1,2,2,2]{3,2,1,0:T(2,128)S(1)}, s32[1,2,2,2]{3,2,1,0:T(2,128)}, u32[]{:S(2)}) copy-start(s32[1,2,2,2]{3,2,1,0:T(2,128)} %param.9) | copy-start | bytes 100
  106.8 81.9 %all-to-all-start = ((bf16[16,256,256]{2,1,0:T(8,128)(2,1)}), bf16[16,256,256]{2,1,0:T(8,128)(2,1)S(1)}, u32[]{:S(2)}, u32[]{:S(2)}) async-start(bf16[16,256,256]{2,1,0:T(8,128)(2,1)} %tile.2), calls=%async_computation | async-start | bytes 4194304 | tf_op jit(solution)/shard_map/all_to_all | solution.py:15
  192.9 28.2 %all-to-all-start.3 = ((bf16[16,64,256]{2,1,0:T(8,128)(2,1)}), bf16[16,64,256]{2,1,0:T(8,128)(2,1)S(1)}, u32[]{:S(2)}, u32[]{:S(2)}) async-start(bf16[16,64,256]{2,1,0:T(8,128)(2,1)} %bitcast.28), calls=%async_computation.3 | async-start | bytes 1048576 | tf_op jit(solution)/shard_map/all_to_all | solution.py:53
  221.1 58.3 %all-to-all-start.2 = ((bf16[32,256,128]{1,2,0:T(8,128)(2,1)}), bf16[32,256,128]{1,2,0:T(8,128)(2,1)S(1)}, u32[]{:S(2)}, u32[]{:S(2)}) async-start(bf16[32,256,128]{1,2,0:T(8,128)(2,1)} %bitcast.105), calls=%async_computation.2 | async-start | bytes 4194304 | tf_op jit(solution)/shard_map/all_to_all | solution.py:46
  279.4 53.6 %all-to-all-start.1 = ((bf16[32,256,128]{1,2,0:T(8,128)(2,1)}), bf16[32,256,128]{1,2,0:T(8,128)(2,1)}, u32[]{:S(2)}, u32[]{:S(2)}) async-start(bf16[32,256,128]{1,2,0:T(8,128)(2,1)} %bitcast.106), calls=%async_computation.1 | async-start | bytes 4194304 | tf_op jit(solution)/shard_map/all_to_all | solution.py:46
  333.8 23.4 %all-to-all-start.4 = ((bf16[16,64,256]{2,1,0:T(8,128)(2,1)}), bf16[16,64,256]{2,1,0:T(8,128)(2,1)S(1)}, u32[]{:S(2)}, u32[]{:S(2)}) async-start(bf16[16,64,256]{2,1,0:T(8,128)(2,1)} %broadcast_in_dim.11), calls=%async_computation.4 | async-start | bytes 1048576 | tf_op jit(solution)/shard_map/all_to_all | solution.py:56
  339.8 2.2 copy-start.1
  339.8 2.2 copy-start.2
  342.1 16.0 %collective-permute-start = (bf16[1,128,256]{2,1,0:T(8,128)(2,1)S(1)}, bf16[1,128,256]{2,1,0:T(8,128)(2,1)S(1)}, u32[]{:S(2)}, u32[]{:S(2)}) collective-permute-start(bf16[1,128,256]{2,1,0:T(8,128)(2,1)S(1)} %get-tuple-element.53), channel_id=1, source_target_pairs={{0,32},{32,64},{64,96},{96,128},{128,160},{160,192},{192,224},{224... | collective-permute-start | bytes 196616 | tf_op jit(solution)/shard_map/ppermute | solution.py:20
  343.7 14.4 %collective-permute-start.1 = (bf16[1,128,256]{2,1,0:T(8,128)(2,1)S(1)}, bf16[1,128,256]{2,1,0:T(8,128)(2,1)S(1)}, u32[]{:S(2)}, u32[]{:S(2)}) collective-permute-start(bf16[1,128,256]{2,1,0:T(8,128)(2,1)S(1)} %get-tuple-element.52), channel_id=1, source_target_pairs={{0,480},{32,0},{64,32},{96,64},{128,96},{160,128},{192,160},{224,1... | collective-permute-start | bytes 196616 | tf_op jit(solution)/shard_map/ppermute | solution.py:20
Sparse Core Ops, SparseCore 0:
  11.0 90.6 all-gather.4
  104.8 80.8 all-gather.6
